TPU v7x, 512 devices: a whole 4x8x8 slice. The times are simulated.
512 devices in a mesh: ctx: 128 (over x, z, y_lo, core), head: 4 (over y_hi).
Axes of the slice: x: 4, y: 8 (y_hi: 4, y_lo: 2; y = y_hi * 2 + y_lo), z: 8, core: 2. Of those that a mesh axis runs over, the one named last changes fastest.
Arguments:
- queries: bfloat16 [32768, 2048], P('ctx', 'head'), may hold values from -8 to 8
- keys: bfloat16 [32768, 2048], P('ctx', 'head'), may hold values from -8 to 8
- values: bfloat16 [32768, 2048], P('ctx', 'head'), may hold values from -6 to 6
- out_grad: bfloat16 [32768, 2048], P('ctx', 'head'), may hold values from -6 to 6
Outputs:
- attended: bfloat16 [32768, 2048], P('ctx', 'head')
- query_grad: bfloat16 [32768, 2048], P('ctx', 'head')
- key_grad: bfloat16 [32768, 2048], P('ctx', 'head')
- value_grad: bfloat16 [32768, 2048], P('ctx', 'head')
All inputs are finite; a program needn't handle non-finite values.
Results may differ from a plain program's by a relative error of at most 0.017.
Values may be sent and summed in bfloat16 or wider, within the bound.
No kernel may reach another device: no remote copies, remote signals or barrier semaphores. Data moves between devices by JAX's collectives and lax.ppermute only.
A program may use at most 64 MiB of HBM per device.

v0:
```python
import math
import jax
import jax.numpy as jnp
from jax import lax
from jax.sharding import PartitionSpec as P

HD = 128
STRIDE = 128
SUMMARY = 4


def split_heads(matrix):
    blocks = matrix.shape[0] // STRIDE
    half_heads = matrix.shape[1] // (2 * HD)
    shaped = matrix.reshape(blocks, STRIDE, matrix.shape[1] // (4 * HD), 4, HD)
    fixed = shaped[:, :, :, :2].reshape(blocks, STRIDE, half_heads, HD)
    strided = shaped[:, :, :, 2:].reshape(blocks, STRIDE, half_heads, HD)
    return (fixed, strided)


def join_heads(fixed, strided):
    blocks, positions, half_heads, head_dim = fixed.shape
    paired = jnp.concatenate(
        [
            fixed.reshape(blocks, positions, half_heads // 2, 2, head_dim),
            strided.reshape(blocks, positions, half_heads // 2, 2, head_dim),
        ],
        axis=3,
    )
    return paired.reshape(blocks * positions, 2 * half_heads * head_dim)


def fixed_heads(query, key_rows, value_rows, grad_rows, scaling):
    blocks_here, positions, half_heads, head_dim = query.shape
    summary_keys = key_rows[:, positions - SUMMARY :]
    summary_values = value_rows[:, positions - SUMMARY :]
    every_key, every_value = (
        lax.all_gather(summary_keys, "ctx", axis=0, tiled=True),
        lax.all_gather(summary_values, "ctx", axis=0, tiled=True),
    )
    summary_count = every_key.shape[0] * SUMMARY
    flat_keys = every_key.reshape(summary_count, half_heads, head_dim)
    flat_values = every_value.reshape(summary_count, half_heads, head_dim)
    block_ids = lax.axis_index("ctx") * blocks_here + jnp.arange(blocks_here, dtype=jnp.int32)
    summary_block = jnp.arange(summary_count, dtype=jnp.int32) // SUMMARY
    earlier = (summary_block[None, :] < block_ids[:, None])[:, None, None, :]
    causal = (jnp.arange(positions)[:, None] >= jnp.arange(positions)[None, :])[None, None]
    local_scores = (
        jnp.einsum("bqgd,bkgd->bgqk", query, key_rows, preferred_element_type=jnp.float32) * scaling
    )
    summary_scores = (
        jnp.einsum("bqgd,mgd->bgqm", query, flat_keys, preferred_element_type=jnp.float32) * scaling
    )
    local_scores = jnp.where(causal, local_scores, -jnp.inf)
    summary_scores = jnp.where(earlier, summary_scores, -jnp.inf)
    row_max = jnp.maximum(jnp.max(local_scores, axis=-1), jnp.max(summary_scores, axis=-1))[
        ..., None
    ]
    local_raised = jnp.exp(local_scores - row_max)
    summary_raised = jnp.exp(summary_scores - row_max)
    totals = jnp.sum(local_raised, axis=-1, keepdims=True) + jnp.sum(
        summary_raised, axis=-1, keepdims=True
    )
    local_weights = local_raised / totals
    summary_weights = summary_raised / totals
    local_low = local_weights.astype(jnp.bfloat16)
    summary_low = summary_weights.astype(jnp.bfloat16)
    attended = (
        jnp.einsum("bgqk,bkgd->bqgd", local_low, value_rows, preferred_element_type=jnp.float32)
        + jnp.einsum("bgqm,mgd->bqgd", summary_low, flat_values, preferred_element_type=jnp.float32)
    ).astype(jnp.bfloat16)
    local_dweights = jnp.einsum(
        "bqgd,bkgd->bgqk", grad_rows, value_rows, preferred_element_type=jnp.float32
    )
    summary_dweights = jnp.einsum(
        "bqgd,mgd->bgqm", grad_rows, flat_values, preferred_element_type=jnp.float32
    )
    row_delta = jnp.sum(grad_rows.astype(jnp.float32) * attended.astype(jnp.float32), axis=-1)
    row_delta = jnp.transpose(row_delta, (0, 2, 1))[..., None]
    local_dscores = (local_weights * (local_dweights - row_delta)).astype(jnp.bfloat16)
    summary_dscores = (summary_weights * (summary_dweights - row_delta)).astype(jnp.bfloat16)
    query_grad = (
        jnp.einsum("bgqk,bkgd->bqgd", local_dscores, key_rows, preferred_element_type=jnp.float32)
        + jnp.einsum(
            "bgqm,mgd->bqgd", summary_dscores, flat_keys, preferred_element_type=jnp.float32
        )
    ) * scaling
    key_grad = (
        jnp.einsum("bgqk,bqgd->bkgd", local_dscores, query, preferred_element_type=jnp.float32)
        * scaling
    )
    value_grad = jnp.einsum(
        "bgqk,bqgd->bkgd", local_low, grad_rows, preferred_element_type=jnp.float32
    )
    key_terms = (
        jnp.einsum("bgqm,bqgd->mgd", summary_dscores, query, preferred_element_type=jnp.float32)
        * scaling
    )
    value_terms = jnp.einsum(
        "bgqm,bqgd->mgd", summary_low, grad_rows, preferred_element_type=jnp.float32
    )
    shares = lax.psum_scatter(
        jnp.stack([key_terms, value_terms], axis=1), "ctx", scatter_dimension=0, tiled=True
    )
    shares = shares.reshape(blocks_here, SUMMARY, 2, half_heads, head_dim)
    key_grad = key_grad.at[:, positions - SUMMARY :].add(shares[:, :, 0])
    value_grad = value_grad.at[:, positions - SUMMARY :].add(shares[:, :, 1])
    return (
        attended,
        query_grad.astype(jnp.bfloat16),
        key_grad.astype(jnp.bfloat16),
        value_grad.astype(jnp.bfloat16),
    )


def strided_heads(query, key_rows, value_rows, grad_rows, scaling):
    query_all = lax.all_to_all(query, "ctx", split_axis=1, concat_axis=0, tiled=True)
    keys_all = lax.all_to_all(key_rows, "ctx", split_axis=1, concat_axis=0, tiled=True)
    values_all = lax.all_to_all(value_rows, "ctx", split_axis=1, concat_axis=0, tiled=True)
    grads_all = lax.all_to_all(grad_rows, "ctx", split_axis=1, concat_axis=0, tiled=True)
    blocks = query_all.shape[0]
    causal = (jnp.arange(blocks)[:, None] >= jnp.arange(blocks)[None, :])[None, None]
    scores = (
        jnp.einsum("brgd,crgd->rgbc", query_all, keys_all, preferred_element_type=jnp.float32)
        * scaling
    )
    scores = jnp.where(causal, scores, -jnp.inf)
    row_max = jnp.max(scores, axis=-1, keepdims=True)
    raised = jnp.exp(scores - row_max)
    weights = raised / jnp.sum(raised, axis=-1, keepdims=True)
    weights_low = weights.astype(jnp.bfloat16)
    attended = jnp.einsum(
        "rgbc,crgd->brgd", weights_low, values_all, preferred_element_type=jnp.float32
    ).astype(jnp.bfloat16)
    dweights = jnp.einsum(
        "brgd,crgd->rgbc", grads_all, values_all, preferred_element_type=jnp.float32
    )
    row_delta = jnp.sum(grads_all.astype(jnp.float32) * attended.astype(jnp.float32), axis=-1)
    row_delta = jnp.transpose(row_delta, (1, 2, 0))[..., None]
    dscores = (weights * (dweights - row_delta)).astype(jnp.bfloat16)
    query_grad = (
        jnp.einsum("rgbc,crgd->brgd", dscores, keys_all, preferred_element_type=jnp.float32)
        * scaling
    ).astype(jnp.bfloat16)
    key_grad = (
        jnp.einsum("rgbc,brgd->crgd", dscores, query_all, preferred_element_type=jnp.float32)
        * scaling
    ).astype(jnp.bfloat16)
    value_grad = jnp.einsum(
        "rgbc,brgd->crgd", weights_low, grads_all, preferred_element_type=jnp.float32
    ).astype(jnp.bfloat16)
    return (
        lax.all_to_all(attended, "ctx", split_axis=0, concat_axis=1, tiled=True),
        lax.all_to_all(query_grad, "ctx", split_axis=0, concat_axis=1, tiled=True),
        lax.all_to_all(key_grad, "ctx", split_axis=0, concat_axis=1, tiled=True),
        lax.all_to_all(value_grad, "ctx", split_axis=0, concat_axis=1, tiled=True),
    )


def shards(queries, keys, values, out_grad):
    scaling = 1.0 / math.sqrt(HD)
    query_fixed, query_strided = split_heads(queries)
    key_fixed, key_strided = split_heads(keys)
    value_fixed, value_strided = split_heads(values)
    grad_fixed, grad_strided = split_heads(out_grad)
    fixed_out = fixed_heads(query_fixed, key_fixed, value_fixed, grad_fixed, scaling)
    strided_out = strided_heads(query_strided, key_strided, value_strided, grad_strided, scaling)
    return (
        join_heads(fixed_out[0], strided_out[0]),
        join_heads(fixed_out[1], strided_out[1]),
        join_heads(fixed_out[2], strided_out[2]),
        join_heads(fixed_out[3], strided_out[3]),
    )


def solution(mesh):
    return jax.shard_map(
        shards,
        mesh=mesh,
        in_specs=(P("ctx", "head"), P("ctx", "head"), P("ctx", "head"), P("ctx", "head")),
        out_specs=(P("ctx", "head"), P("ctx", "head"), P("ctx", "head"), P("ctx", "head")),
        check_vma=False,
    )
```

profile of v0, /device:TPU:16, one launch (start us, length us, event | category | flops | bytes accessed | tf_op | source)
XLA Modules:
  0.0 909.7 jit_solution(8492532768877551417)
XLA Ops:
  7.3 1.1 reshape.335
  8.8 1.0 reshape.319
  11.0 165.1 %all_gather.7 = bf16[256,4,2,128]{3,1,2,0:T(4,128)(2,1)S(1)} all-gather(bf16[2,4,2,128]{3,1,2,0:T(4,128)(2,1)S(1)} %copy.203), channel_id=1, replica_groups=mesh['ctx'=128,'head'=4] {'ctx'}, dimensions={0}, use_global_device_ids=true | all-gather | bytes 528384 | tf_op jit(solution)/shard_map/all_gather | solution.py:39
  176.2 153.2 %all_gather.6 = bf16[256,4,2,128]{3,1,2,0:T(4,128)(2,1)S(1)} all-gather(bf16[2,4,2,128]{3,1,2,0:T(4,128)(2,1)S(1)} %slice.111), channel_id=1, replica_groups=mesh['ctx'=128,'head'=4] {'ctx'}, dimensions={0}, use_global_device_ids=true | all-gather | bytes 528384 | tf_op jit(solution)/shard_map/all_gather | solution.py:38
  331.5 0.9 multiply_reduce_fusion.1
  333.8 1.5 pad_maximum_fusion
  336.1 6.2 all-to-all-start
  343.0 10.3 %all-to-all-done = bf16[2,128,2,128]{3,2,0,1:T(2,128)(2,1)S(1)} async-done(((bf16[2,128,2,128]{3,2,0,1:T(2,128)(2,1)}), bf16[2,128,2,128]{3,2,0,1:T(2,128)(2,1)S(1)}, u32[]{:S(2)}, u32[]{:S(2)}) %all-to-all-start) | async-done | bytes 131104 | tf_op jit(solution)/shard_map/all_to_all | solution.py:117
  353.3 6.2 all-to-all-start.1
  360.2 10.3 %all-to-all-done.1 = bf16[2,128,2,128]{3,2,0,1:T(2,128)(2,1)S(1)} async-done(((bf16[2,128,2,128]{3,2,0,1:T(2,128)(2,1)}), bf16[2,128,2,128]{3,2,0,1:T(2,128)(2,1)S(1)}, u32[]{:S(2)}, u32[]{:S(2)}) %all-to-all-start.1) | async-done | bytes 131104 | tf_op jit(solution)/shard_map/all_to_all | solution.py:118
  370.6 6.4 all-to-all-start.2
  377.7 10.2 %all-to-all-done.2 = bf16[2,128,2,128]{3,2,0,1:T(2,128)(2,1)S(1)} async-done(((bf16[2,128,2,128]{3,2,0,1:T(2,128)(2,1)}), bf16[2,128,2,128]{3,2,0,1:T(2,128)(2,1)S(1)}, u32[]{:S(2)}, u32[]{:S(2)}) %all-to-all-start.2) | async-done | bytes 131104 | tf_op jit(solution)/shard_map/all_to_all | solution.py:119
  387.9 6.2 all-to-all-start.4
  394.9 10.2 %all-to-all-done.4 = bf16[2,128,2,128]{3,2,0,1:T(2,128)(2,1)S(1)} async-done(((bf16[2,128,2,128]{3,2,0,1:T(2,128)(2,1)}), bf16[2,128,2,128]{3,2,0,1:T(2,128)(2,1)S(1)}, u32[]{:S(2)}, u32[]{:S(2)}) %all-to-all-start.4) | async-done | bytes 131104 | tf_op jit(solution)/shard_map/all_to_all | solution.py:120
  405.7 2.0 fusion.64
  407.7 1.3 multiply_reduce_fusion
  409.0 1.3 fusion.11
  411.3 6.2 all-to-all-start.6
  418.0 0.8 copy.234
  418.8 9.7 %all-to-all-done.6 = bf16[256,1,2,128]{3,2,1,0:T(2,128)(2,1)S(1)} async-done(((bf16[256,1,2,128]{3,2,1,0:T(2,128)(2,1)}), bf16[256,1,2,128]{3,2,1,0:T(2,128)(2,1)S(1)}, u32[]{:S(2)}, u32[]{:S(2)}) %all-to-all-start.6) | async-done | bytes 131104 | tf_op jit(solution)/shard_map/all_to_all | solution.py:155
  428.5 6.2 all-to-all-start.5
  434.9 1.3 fusion.24
  436.1 0.8 copy.248
  436.9 8.8 all-to-all-done.5
  445.7 6.4 all-to-all-start.7
  453.4 9.7 %all-to-all-done.7 = bf16[256,1,2,128]{3,2,1,0:T(2,128)(2,1)S(1)} async-done(((bf16[256,1,2,128]{3,2,1,0:T(2,128)(2,1)}), bf16[256,1,2,128]{3,2,1,0:T(2,128)(2,1)S(1)}, u32[]{:S(2)}, u32[]{:S(2)}) %all-to-all-start.7) | async-done | bytes 131104 | tf_op jit(solution)/shard_map/all_to_all | solution.py:156
  463.2 6.2 all-to-all-start.3
  470.0 10.4 %all-to-all-done.3 = bf16[256,1,2,128]{3,2,1,0:T(2,128)(2,1)S(1)} async-done(((bf16[256,1,2,128]{3,2,1,0:T(2,128)(2,1)}), bf16[256,1,2,128]{3,2,1,0:T(2,128)(2,1)S(1)}, u32[]{:S(2)}, u32[]{:S(2)}) %all-to-all-start.3) | async-done | bytes 131104 | tf_op jit(solution)/shard_map/all_to_all | solution.py:153
  481.0 0.9 copy_bitcast_fusion.2
  481.9 417.3 %reduce-scatter.2.cloned.1.call-done = f32[8,2,2,128]{3,0,2,1:T(8,128)} async-done(((f32[1024,2,2,128]{3,0,2,1:T(8,128)}), f32[8,2,2,128]{3,0,2,1:T(8,128)}) %reduce-scatter.2.cloned.1.call-update) | async-done | bytes 16400 | tf_op jit(solution)/shard_map/reduce_scatter | solution.py:102
  900.5 1.2 scatter-add.6
  902.0 0.9 copy_bitcast_fusion
  (85 shorter events, 15.4 us)
Async XLA Ops:
  7.2 2.9 copy-start
  7.2 3.2 copy-start.1
  7.2 892.0 %reduce-scatter.2.cloned.1.call-start = ((), (), s32[]{:S(2)}) async-start(), calls=%async_computation.9 | async-start | bytes 2113536 | tf_op jit(solution)/shard_map/reduce_scatter | solution.py:102
  336.1 17.2 %all-to-all-start = ((bf16[2,128,2,128]{3,2,0,1:T(2,128)(2,1)}), bf16[2,128,2,128]{3,2,0,1:T(2,128)(2,1)S(1)}, u32[]{:S(2)}, u32[]{:S(2)}) async-start(bf16[2,128,2,128]{3,2,0,1:T(2,128)(2,1)} %copy.207), calls=%async_computation | async-start | bytes 262144 | tf_op jit(solution)/shard_map/all_to_all | solution.py:117
  353.3 17.3 %all-to-all-start.1 = ((bf16[2,128,2,128]{3,2,0,1:T(2,128)(2,1)}), bf16[2,128,2,128]{3,2,0,1:T(2,128)(2,1)S(1)}, u32[]{:S(2)}, u32[]{:S(2)}) async-start(bf16[2,128,2,128]{3,2,0,1:T(2,128)(2,1)} %copy.209), calls=%async_computation.1 | async-start | bytes 262144 | tf_op jit(solution)/shard_map/all_to_all | solution.py:118
  370.6 17.3 %all-to-all-start.2 = ((bf16[2,128,2,128]{3,2,0,1:T(2,128)(2,1)}), bf16[2,128,2,128]{3,2,0,1:T(2,128)(2,1)S(1)}, u32[]{:S(2)}, u32[]{:S(2)}) async-start(bf16[2,128,2,128]{3,2,0,1:T(2,128)(2,1)} %copy.211), calls=%async_computation.2 | async-start | bytes 262144 | tf_op jit(solution)/shard_map/all_to_all | solution.py:119
  387.9 17.3 %all-to-all-start.4 = ((bf16[2,128,2,128]{3,2,0,1:T(2,128)(2,1)}), bf16[2,128,2,128]{3,2,0,1:T(2,128)(2,1)S(1)}, u32[]{:S(2)}, u32[]{:S(2)}) async-start(bf16[2,128,2,128]{3,2,0,1:T(2,128)(2,1)} %copy.227), calls=%async_computation.4 | async-start | bytes 262144 | tf_op jit(solution)/shard_map/all_to_all | solution.py:120
  405.7 4.6 copy-start.2
  410.5 24.4 %copy-start.3 = (bf16[128,2,1,2,128]{4,1,0,3,2:T(2,128)(2,1)S(1)}, bf16[128,2,1,2,128]{4,1,0,3,2:T(2,128)(2,1)}, u32[]{:S(2)}) copy-start(bf16[128,2,1,2,128]{4,1,0,3,2:T(2,128)(2,1)} %copy-done.2) | copy-start | bytes 393220
  411.3 17.2 %all-to-all-start.6 = ((bf16[256,1,2,128]{3,2,1,0:T(2,128)(2,1)}), bf16[256,1,2,128]{3,2,1,0:T(2,128)(2,1)S(1)}, u32[]{:S(2)}, u32[]{:S(2)}) async-start(bf16[256,1,2,128]{3,2,1,0:T(2,128)(2,1)} %copy.242), calls=%async_computation.7 | async-start | bytes 262144 | tf_op jit(solution)/shard_map/all_to_all | solution.py:155
  428.5 17.3 %all-to-all-start.5 = ((bf16[256,1,2,128]{3,2,1,0:T(2,128)(2,1)}), bf16[256,1,2,128]{3,2,1,0:T(2,128)(2,1)S(1)}, u32[]{:S(2)}, u32[]{:S(2)}) async-start(bf16[256,1,2,128]{3,2,1,0:T(2,128)(2,1)} %copy.234), calls=%async_computation.5 | async-start | bytes 262144 | tf_op jit(solution)/shard_map/all_to_all | solution.py:154
  445.7 17.4 %all-to-all-start.7 = ((bf16[256,1,2,128]{3,2,1,0:T(2,128)(2,1)}), bf16[256,1,2,128]{3,2,1,0:T(2,128)(2,1)S(1)}, u32[]{:S(2)}, u32[]{:S(2)}) async-start(bf16[256,1,2,128]{3,2,1,0:T(2,128)(2,1)} %copy.248), calls=%async_computation.8 | async-start | bytes 262144 | tf_op jit(solution)/shard_map/all_to_all | solution.py:156
  453.4 27.4 %copy-start.4 = (bf16[2,128,2,128]{1,3,2,0:T(8,128)(2,1)S(1)}, bf16[2,128,2,128]{1,3,2,0:T(8,128)(2,1)}, u32[]{:S(2)}) copy-start(bf16[2,128,2,128]{1,3,2,0:T(8,128)(2,1)} %get-tuple-element.49) | copy-start | bytes 393220
  463.2 17.3 %all-to-all-start.3 = ((bf16[256,1,2,128]{3,2,1,0:T(2,128)(2,1)}), bf16[256,1,2,128]{3,2,1,0:T(2,128)(2,1)S(1)}, u32[]{:S(2)}, u32[]{:S(2)}) async-start(bf16[256,1,2,128]{3,2,1,0:T(2,128)(2,1)} %copy.215), calls=%async_computation.3 | async-start | bytes 262144 | tf_op jit(solution)/shard_map/all_to_all | solution.py:153
Sparse Core Ops, SparseCore 0:
  335.5 563.6 reduce-scatter.1
where the time goes:
time: 911 us; the launch traced here: 910 us
  waiting for transfers between devices  497 us (55%)
  blocking collectives  318 us (35%)
  starting transfers between devices  49.8 us (5%)
  local copies, waits for them, and re-layouts  15.7 us (2%)
  between operations  14.6 us (2%)
  matrix products  11.1 us (1%)
    reduce_scatter x1, waiting for transfers between devices, fixed_heads(): lax.psum_scatter(jnp.stack([key_terms, value_terms], axis=1), 'ctx', scat...  417 us
    all_gather x1, blocking collectives, fixed_heads(): lax.all_gather(summary_values, 'ctx', axis=0, tiled=True)  165 us
    all_gather x1, blocking collectives, fixed_heads(): lax.all_gather(summary_keys, 'ctx', axis=0, tiled=True)  153 us
  transfers between devices with their start and end apart: 9, of which 9 were waited for; matrix products, arithmetic and copies ran while one was open for 2% of the time, Pallas kernels for 0%

commit v1 on v0

--- a/solution.py
+++ b/solution.py
@@ -36,7 +36,9 @@
     summary_values = value_rows[:, positions - SUMMARY :]
     every_key, every_value = (
         lax.all_gather(summary_keys, "ctx", axis=0, tiled=True),
-        lax.all_gather(summary_values, "ctx", axis=0, tiled=True),
+        jnp.concatenate(
+            lax.all_to_all(jnp.stack([summary_values] * lax.axis_size("ctx")), "ctx", 0, 0), axis=0
+        ),
     )
     summary_count = every_key.shape[0] * SUMMARY
     flat_keys = every_key.reshape(summary_count, half_heads, head_dim)

time: 911 us -> 804 us (0.88)
  blocking collectives: 318 us -> 159 us
  waiting for transfers between devices: 497 us -> 528 us
  starting transfers between devices: 49.8 us -> 67.4 us
    all_gather x1 -> x0, blocking collectives: 165 us -> none  [fixed_heads(): lax.all_gather(summary_values, 'ctx', axis=0, tiled=True)]
    reduce_scatter x1, waiting for transfers between devices: 417 us -> 453 us  [fixed_heads(): lax.psum_scatter(jnp.stack([key_terms, value_terms], axis=1), 'ctx', scat...]
    all_to_all x0 -> x1, starting transfers between devices: none -> 16.6 us  [fixed_heads(): lax.all_to_all(jnp.stack([summary_values] * lax.axis_size('ctx')), 'ctx',...]
  transfers between devices with their start and end apart: 9 -> 10, of which waited for: 9 -> 9; matrix products, arithmetic and copies ran while one was open for 2% -> 3% of each run, Pallas kernels for 0% -> 0%
where the time goes in v1:
time: 804 us; the launch traced here: 803 us
  waiting for transfers between devices  528 us (66%)
  blocking collectives  159 us (20%)
  starting transfers between devices  67.4 us (8%)
  local copies, waits for them, and re-layouts  21.2 us (3%)
  between operations  14.8 us (2%)
  matrix products  8.9 us (1%)
    reduce_scatter x1, waiting for transfers between devices, fixed_heads(): lax.psum_scatter(jnp.stack([key_terms, value_terms], axis=1), 'ctx', scat...  453 us
    all_gather x1, blocking collectives, fixed_heads(): lax.all_gather(summary_keys, 'ctx', axis=0, tiled=True)  159 us
    all_to_all x1, starting transfers between devices, fixed_heads(): lax.all_to_all(jnp.stack([summary_values] * lax.axis_size('ctx')), 'ctx',...  16.6 us
  transfers between devices with their start and end apart: 10, of which 9 were waited for; matrix products, arithmetic and copies ran while one was open for 3% of the time, Pallas kernels for 0%

profile of v1, /device:TPU:16, one launch (start us, length us, event | category | flops | bytes accessed | tf_op | source)
XLA Modules:
  0.0 803.0 jit_solution(7046625186271416631)
XLA Ops:
  7.2 1.1 reshape.323
  9.5 1.0 stack.8
  10.4 16.6 %all-to-all-start = ((bf16[128,2,4,2,128]{4,2,1,3,0:T(4,128)(2,1)}), bf16[128,2,4,2,128]{4,2,1,3,0:T(4,128)(2,1)}, u32[]{:S(2)}, u32[]{:S(2)}) async-start(bf16[128,2,4,2,128]{4,2,1,3,0:T(4,128)(2,1)} %stack.8), calls=%async_computation | async-start | bytes 1048576 | tf_op jit(solution)/shard_map/all_to_all | solution.py:40
  28.6 158.9 %all_gather.3 = bf16[256,4,2,128]{3,1,2,0:T(4,128)(2,1)S(1)} all-gather(bf16[2,4,2,128]{3,1,2,0:T(4,128)(2,1)S(1)} %slice.111), channel_id=1, replica_groups=mesh['ctx'=128,'head'=4] {'ctx'}, dimensions={0}, use_global_device_ids=true | all-gather | bytes 528384 | tf_op jit(solution)/shard_map/all_gather | solution.py:38
  187.7 0.9 fusion.65
  191.8 1.0 fusion.32
  193.2 1.4 convolution_bitcast_fusion
  194.6 7.2 all-to-all-start.1
  201.9 1.3 copy.205
  206.0 6.5 all-to-all-done.1
  212.6 6.4 all-to-all-start.2
  219.0 1.5 pad_maximum_fusion
  220.5 0.9 copy-done.6
  222.1 7.8 all-to-all-done.2
  229.9 6.2 all-to-all-start.3
  236.8 10.3 %all-to-all-done.3 = bf16[2,128,2,128]{3,2,0,1:T(2,128)(2,1)S(1)} async-done(((bf16[2,128,2,128]{3,2,0,1:T(2,128)(2,1)}), bf16[2,128,2,128]{3,2,0,1:T(2,128)(2,1)S(1)}, u32[]{:S(2)}, u32[]{:S(2)}) %all-to-all-start.3) | async-done | bytes 131104 | tf_op jit(solution)/shard_map/all_to_all | solution.py:121
  247.1 6.2 all-to-all-start.5
  253.3 1.0 copy.209
  254.4 9.9 %all-to-all-done.5 = bf16[2,128,2,128]{3,2,0,1:T(2,128)(2,1)S(1)} async-done(((bf16[2,128,2,128]{3,2,0,1:T(2,128)(2,1)}), bf16[2,128,2,128]{3,2,0,1:T(2,128)(2,1)S(1)}, u32[]{:S(2)}, u32[]{:S(2)}) %all-to-all-start.5) | async-done | bytes 131104 | tf_op jit(solution)/shard_map/all_to_all | solution.py:122
  266.7 6.2 all-to-all-start.7
  274.0 9.9 %all-to-all-done.7 = bf16[256,1,2,128]{3,2,1,0:T(2,128)(2,1)S(1)} async-done(((bf16[256,1,2,128]{3,2,1,0:T(2,128)(2,1)}), bf16[256,1,2,128]{3,2,1,0:T(2,128)(2,1)S(1)}, u32[]{:S(2)}, u32[]{:S(2)}) %all-to-all-start.7) | async-done | bytes 131104 | tf_op jit(solution)/shard_map/all_to_all | solution.py:157
  283.9 6.2 all-to-all-start.6
  291.1 9.9 %all-to-all-done.6 = bf16[256,1,2,128]{3,2,1,0:T(2,128)(2,1)S(1)} async-done(((bf16[256,1,2,128]{3,2,1,0:T(2,128)(2,1)}), bf16[256,1,2,128]{3,2,1,0:T(2,128)(2,1)S(1)}, u32[]{:S(2)}, u32[]{:S(2)}) %all-to-all-start.6) | async-done | bytes 131104 | tf_op jit(solution)/shard_map/all_to_all | solution.py:156
  301.1 6.4 all-to-all-start.8
  308.3 10.2 %all-to-all-done.8 = bf16[256,1,2,128]{3,2,1,0:T(2,128)(2,1)S(1)} async-done(((bf16[256,1,2,128]{3,2,1,0:T(2,128)(2,1)}), bf16[256,1,2,128]{3,2,1,0:T(2,128)(2,1)S(1)}, u32[]{:S(2)}, u32[]{:S(2)}) %all-to-all-start.8) | async-done | bytes 131104 | tf_op jit(solution)/shard_map/all_to_all | solution.py:158
  318.5 6.2 all-to-all-start.4
  325.1 10.5 %all-to-all-done.4 = bf16[256,1,2,128]{3,2,1,0:T(2,128)(2,1)S(1)} async-done(((bf16[256,1,2,128]{3,2,1,0:T(2,128)(2,1)}), bf16[256,1,2,128]{3,2,1,0:T(2,128)(2,1)S(1)}, u32[]{:S(2)}, u32[]{:S(2)}) %all-to-all-start.4) | async-done | bytes 131104 | tf_op jit(solution)/shard_map/all_to_all | solution.py:155
  335.8 1.1 fusion.20
  338.4 0.9 copy_bitcast_fusion.2
  339.3 453.1 %reduce-scatter.2.cloned.1.call-done = f32[8,2,2,128]{3,0,2,1:T(8,128)} async-done(((f32[1024,2,2,128]{3,0,2,1:T(8,128)}), f32[8,2,2,128]{3,0,2,1:T(8,128)}) %reduce-scatter.2.cloned.1.call-update) | async-done | bytes 16400 | tf_op jit(solution)/shard_map/reduce_scatter | solution.py:104
  793.7 1.2 scatter-add.6
  795.3 0.9 copy_bitcast_fusion
  (113 shorter events, 19.6 us)
Async XLA Ops:
  7.2 19.9 %copy-start.8 = (bf16[256,512]{1,0:T(8,128)(2,1)S(1)}, bf16[256,512]{1,0:T(8,128)(2,1)}, u32[]{:S(2)}) copy-start(bf16[256,512]{1,0:T(8,128)(2,1)} %param.8) | copy-start | bytes 786436
  7.2 20.1 %copy-start.9 = (bf16[256,512]{1,0:T(8,128)(2,1)S(1)}, bf16[256,512]{1,0:T(8,128)(2,1)}, u32[]{:S(2)}) copy-start(bf16[256,512]{1,0:T(8,128)(2,1)} %param.9) | copy-start | bytes 786436
  9.2 17.8 %copy-start.3 = (bf16[2,128,1,2,128]{1,4,3,0,2:T(8,128)(2,1)}, bf16[2,128,1,2,128]{1,4,3,0,2:T(8,128)(2,1)S(1)}, u32[]{:S(2)}) copy-start(bf16[2,128,1,2,128]{1,4,3,0,2:T(8,128)(2,1)S(1)} %copy.286) | copy-start | bytes 393220
  9.3 18.3 %copy-start.10 = (bf16[256,512]{1,0:T(8,128)(2,1)S(1)}, bf16[256,512]{1,0:T(8,128)(2,1)}, u32[]{:S(2)}) copy-start(bf16[256,512]{1,0:T(8,128)(2,1)} %param.11) | copy-start | bytes 786436
  10.4 184.2 %all-to-all-start = ((bf16[128,2,4,2,128]{4,2,1,3,0:T(4,128)(2,1)}), bf16[128,2,4,2,128]{4,2,1,3,0:T(4,128)(2,1)}, u32[]{:S(2)}, u32[]{:S(2)}) async-start(bf16[128,2,4,2,128]{4,2,1,3,0:T(4,128)(2,1)} %stack.8), calls=%async_computation | async-start | bytes 1048576 | tf_op jit(solution)/shard_map/all_to_all | solution.py:40
  187.6 1.8 copy-start.1
  194.6 17.9 %all-to-all-start.1 = ((bf16[2,128,2,128]{3,2,0,1:T(2,128)(2,1)}), bf16[2,128,2,128]{3,2,0,1:T(2,128)(2,1)}, u32[]{:S(2)}, u32[]{:S(2)}) async-start(bf16[2,128,2,128]{3,2,0,1:T(2,128)(2,1)} %copy.208), calls=%async_computation.1 | async-start | bytes 262144 | tf_op jit(solution)/shard_map/all_to_all | solution.py:119
  201.9 1.7 copy-start.4
  201.9 1.7 copy-start.11
  201.9 1.7 copy-start.13
  204.4 0.6 copy-start.16
  205.6 13.4 %copy-start = (f32[1024,1,2,128]{3,0,2,1:T(8,128)S(1)}, f32[1024,1,2,128]{3,0,2,1:T(8,128)}, u32[]{:S(2)}) copy-start(f32[1024,1,2,128]{3,0,2,1:T(8,128)} %convolution_bitcast_fusion) | copy-start | bytes 3145732
  212.6 17.3 %all-to-all-start.2 = ((bf16[2,128,2,128]{3,2,0,1:T(2,128)(2,1)}), bf16[2,128,2,128]{3,2,0,1:T(2,128)(2,1)S(1)}, u32[]{:S(2)}, u32[]{:S(2)}) async-start(bf16[2,128,2,128]{3,2,0,1:T(2,128)(2,1)} %copy.210), calls=%async_computation.2 | async-start | bytes 262144 | tf_op jit(solution)/shard_map/all_to_all | solution.py:120
  218.9 573.5 %reduce-scatter.2.cloned.1.call-start = ((), (), s32[]{:S(2)}) async-start(), calls=%async_computation.10 | async-start | bytes 2113536 | tf_op jit(solution)/shard_map/reduce_scatter | solution.py:104
  220.4 0.9 copy-start.6
  220.4 15.6 %copy-start.7 = (bf16[2,128,2,128]{3,2,1,0:T(2,128)(2,1)S(1)}, bf16[2,128,2,128]{3,2,1,0:T(2,128)(2,1)}, u32[]{:S(2)}) copy-start(bf16[2,128,2,128]{3,2,1,0:T(2,128)(2,1)} %get-tuple-element.29) | copy-start | bytes 393220
  229.9 17.2 %all-to-all-start.3 = ((bf16[2,128,2,128]{3,2,0,1:T(2,128)(2,1)}), bf16[2,128,2,128]{3,2,0,1:T(2,128)(2,1)S(1)}, u32[]{:S(2)}, u32[]{:S(2)}) async-start(bf16[2,128,2,128]{3,2,0,1:T(2,128)(2,1)} %copy.212), calls=%async_computation.3 | async-start | bytes 262144 | tf_op jit(solution)/shard_map/all_to_all | solution.py:121
  247.1 17.2 %all-to-all-start.5 = ((bf16[2,128,2,128]{3,2,0,1:T(2,128)(2,1)}), bf16[2,128,2,128]{3,2,0,1:T(2,128)(2,1)S(1)}, u32[]{:S(2)}, u32[]{:S(2)}) async-start(bf16[2,128,2,128]{3,2,0,1:T(2,128)(2,1)} %copy.228), calls=%async_computation.5 | async-start | bytes 262144 | tf_op jit(solution)/shard_map/all_to_all | solution.py:122
  266.7 17.2 %all-to-all-start.7 = ((bf16[256,1,2,128]{3,2,1,0:T(2,128)(2,1)}), bf16[256,1,2,128]{3,2,1,0:T(2,128)(2,1)S(1)}, u32[]{:S(2)}, u32[]{:S(2)}) async-start(bf16[256,1,2,128]{3,2,1,0:T(2,128)(2,1)} %copy.243), calls=%async_computation.8 | async-start | bytes 262144 | tf_op jit(solution)/shard_map/all_to_all | solution.py:157
  272.9 51.8 %copy-start.12 = (f32[2,2,128,128]{2,3,1,0:T(8,128)S(1)}, f32[2,2,128,128]{2,3,1,0:T(8,128)}, u32[]{:S(2)}) copy-start(f32[2,2,128,128]{2,3,1,0:T(8,128)} %get-tuple-element.43) | copy-start | bytes 786436
  272.9 51.8 %copy-start.14 = (bf16[2,128,1,2,128]{1,4,3,0,2:T(8,128)(2,1)S(1)}, bf16[2,128,1,2,128]{1,4,3,0,2:T(8,128)(2,1)}, u32[]{:S(2)}) copy-start(bf16[2,128,1,2,128]{1,4,3,0,2:T(8,128)(2,1)} %copy.289) | copy-start | bytes 393220
  283.9 17.2 %all-to-all-start.6 = ((bf16[256,1,2,128]{3,2,1,0:T(2,128)(2,1)}), bf16[256,1,2,128]{3,2,1,0:T(2,128)(2,1)S(1)}, u32[]{:S(2)}, u32[]{:S(2)}) async-start(bf16[256,1,2,128]{3,2,1,0:T(2,128)(2,1)} %copy.235), calls=%async_computation.6 | async-start | bytes 262144 | tf_op jit(solution)/shard_map/all_to_all | solution.py:156
  290.3 45.4 %copy-start.5 = (bf16[2,128,1,2,128]{1,4,3,0,2:T(8,128)(2,1)S(1)}, bf16[2,128,1,2,128]{1,4,3,0,2:T(8,128)(2,1)}, u32[]{:S(2)}) copy-start(bf16[2,128,1,2,128]{1,4,3,0,2:T(8,128)(2,1)} %copy-done.3) | copy-start | bytes 393220
  290.3 45.4 %copy-start.17 = (f32[2,128,2]{1,2,0:T(2,128)S(1)}, f32[2,128,2]{1,2,0:T(2,128)}, u32[]{:S(2)}) copy-start(f32[2,128,2]{1,2,0:T(2,128)} %copy-done.16) | copy-start | bytes 6148
  301.1 17.4 %all-to-all-start.8 = ((bf16[256,1,2,128]{3,2,1,0:T(2,128)(2,1)}), bf16[256,1,2,128]{3,2,1,0:T(2,128)(2,1)S(1)}, u32[]{:S(2)}, u32[]{:S(2)}) async-start(bf16[256,1,2,128]{3,2,1,0:T(2,128)(2,1)} %copy.249), calls=%async_computation.9 | async-start | bytes 262144 | tf_op jit(solution)/shard_map/all_to_all | solution.py:158
  308.3 28.7 %copy-start.2 = (bf16[256,4,2,128]{3,1,0,2:T(4,128)(2,1)S(1)}, bf16[256,4,2,128]{3,1,0,2:T(4,128)(2,1)}, u32[]{:S(2)}) copy-start(bf16[256,4,2,128]{3,1,0,2:T(4,128)(2,1)} %copy-done.1) | copy-start | bytes 1572868
  318.5 17.1 %all-to-all-start.4 = ((bf16[256,1,2,128]{3,2,1,0:T(2,128)(2,1)}), bf16[256,1,2,128]{3,2,1,0:T(2,128)(2,1)S(1)}, u32[]{:S(2)}, u32[]{:S(2)}) async-start(bf16[256,1,2,128]{3,2,1,0:T(2,128)(2,1)} %copy.216), calls=%async_computation.4 | async-start | bytes 262144 | tf_op jit(solution)/shard_map/all_to_all | solution.py:155
  336.9 1.0 copy-start.15
Sparse Core Ops, SparseCore 0:
  222.5 569.8 reduce-scatter.1
